TPU v7x, 256 devices: a whole 4x4x8 slice. The times are simulated.
256 devices in a mesh: rep: 32 (over x, y, core), tp: 8 (over z).
Axes of the slice: x: 4, y: 4, z: 8, core: 2. Of those that a mesh axis runs over, the one named last changes fastest.
Arguments:
- prompt_rows: bfloat16 [20480, 2048], P(('rep', 'tp')), may hold values from -6 to 6
- prompt_pieces: int32 [32, 640], P('rep'), may hold values from 0 to 9, never falling along the last dimension, each value on 1 to 320 neighbouring positions
- decode_rows: bfloat16 [1280, 2048], P('rep'), may hold values from -6 to 6
- request_ages: int32 [1280], P('rep'), may hold values from 2 to 127
- migrate_to: int32 [512, 1], P('rep'), may hold values from 0 to 31, as said below
- past_cache: bfloat16 [1280, 2, 128, 2048], P('rep', None, None, 'tp'), may hold values from -8 to 8
- norm_gain: float32 [2048], replicated, may hold values from 0.5 to 1.5
- norm_bias: float32 [2048], replicated, may hold values from -2 to 2
- qkv_weight: bfloat16 [3, 2048, 2048], P(None, None, 'tp'), may hold values from -0.125 to 0.125
- qkv_bias: float32 [3, 2048], P(None, 'tp'), may hold values from -4 to 4
- out_weight: bfloat16 [2048, 2048], P('tp'), may hold values from -0.125 to 0.125
- out_bias: float32 [2048], replicated, may hold values from -3 to 3
Outputs:
- prompt_out: bfloat16 [20480, 2048], P(('rep', 'tp'))
- prompt_cache: bfloat16 [2, 20480, 2048], P(None, 'rep', 'tp')
- kept_out: bfloat16 [768, 2048], P('rep')
- kept_cache: bfloat16 [768, 2, 128, 2048], P('rep', None, None, 'tp')
- moved_out: bfloat16 [1024, 2048], P('rep')
- moved_cache: bfloat16 [1024, 2, 128, 2048], P('rep', None, None, 'tp')
Inputs may be any that keep to these rules, and one draw needn't show every extreme that they name: `migrate_to`: the 16 requests that leave one replica name 16 different target replicas, and one target replica is named by every replica. `prompt_pieces`: piece numbers never fall along a replica's prompt tokens; a piece has at most 320 tokens, and some piece exactly that many.
All inputs are finite; a program needn't handle non-finite values.
Results may differ from a plain program's by a relative error of at most 0.014.
Values may be sent and summed in bfloat16 or wider, within the bound.
No kernel may reach another device: no remote copies, remote signals or barrier semaphores. Data moves between devices by JAX's collectives and lax.ppermute only.
A program may use at most 128 MiB of HBM per device.

v0:
```python
import jax
import jax.numpy as jnp
from jax import lax
from jax.sharding import PartitionSpec as P

HEAD_DIM = 128
CAP = 1
EPSILON = 1e-05


def layer_norm(values, norm_gain, norm_bias):
    wide = values.astype(jnp.float32)
    center = jnp.mean(wide, axis=-1, keepdims=True)
    spread = jnp.mean(jnp.square(wide - center), axis=-1, keepdims=True)
    scaled = (wide - center) * lax.rsqrt(spread + EPSILON)
    return (scaled * norm_gain + norm_bias).astype(jnp.bfloat16)


def decode_partial(
    rows, cache, live, position, norm_gain, norm_bias, qkv_weight, qkv_bias, out_weight
):
    count = rows.shape[0]
    width = qkv_weight.shape[2]
    heads_here = width // HEAD_DIM
    length = cache.shape[2]
    normed = layer_norm(rows, norm_gain, norm_bias)
    projected = jnp.einsum("rd,cde->cre", normed, qkv_weight, preferred_element_type=jnp.float32)
    queries = (projected[0] + qkv_bias[0]).astype(jnp.bfloat16).reshape(count, heads_here, HEAD_DIM)
    key_new = (projected[1] + qkv_bias[1]).astype(jnp.bfloat16)
    value_new = (projected[2] + qkv_bias[2]).astype(jnp.bfloat16)
    old_keys = cache[:, 0].reshape(count, length, heads_here, HEAD_DIM)
    old_values = cache[:, 1].reshape(count, length, heads_here, HEAD_DIM)
    scale = HEAD_DIM ** (-0.5)
    scores = (
        jnp.einsum("rhe,rlhe->rhl", queries, old_keys, preferred_element_type=jnp.float32) * scale
    )
    own = (
        jnp.sum(
            queries.astype(jnp.float32)
            * key_new.astype(jnp.float32).reshape(count, heads_here, HEAD_DIM),
            axis=-1,
        )
        * scale
    )
    scores = jnp.where(live[:, None, :], scores, -1e30)
    highest = jnp.maximum(jnp.max(scores, axis=-1), own)
    weights = jnp.exp(scores - highest[..., None])
    own_weight = jnp.exp(own - highest)
    total = jnp.sum(weights, axis=-1) + own_weight
    probs = (weights / total[..., None]).astype(jnp.bfloat16)
    own_prob = (own_weight / total).astype(jnp.bfloat16)
    context = jnp.einsum("rhl,rlhe->rhe", probs, old_values, preferred_element_type=jnp.float32)
    context = context + own_prob.astype(jnp.float32)[..., None] * value_new.astype(
        jnp.float32
    ).reshape(count, heads_here, HEAD_DIM)
    context = context.reshape(count, width).astype(jnp.bfloat16)
    partial_value = jnp.dot(context, out_weight, preferred_element_type=jnp.float32)
    written = (jnp.arange(length)[None, :] == position[:, None])[:, :, None]
    new_keys = jnp.where(written, key_new[:, None, :], cache[:, 0])
    new_values = jnp.where(written, value_new[:, None, :], cache[:, 1])
    return (partial_value, jnp.stack([new_keys, new_values], axis=1))


def on_device(
    prompt_rows,
    prompt_pieces,
    decode_rows,
    request_ages,
    migrate_to,
    past_cache,
    norm_gain,
    norm_bias,
    qkv_weight,
    qkv_bias,
    out_weight,
    out_bias,
):
    rep_count = lax.axis_size("rep")
    width = qkv_weight.shape[2]
    heads_here = width // HEAD_DIM
    length = past_cache.shape[2]
    leaving = migrate_to.shape[0]
    staying = decode_rows.shape[0] - leaving
    slot_count = rep_count * CAP
    normed = layer_norm(lax.all_gather(prompt_rows, "tp", axis=0, tiled=True), norm_gain, norm_bias)
    projected = jnp.einsum("rd,cde->cre", normed, qkv_weight, preferred_element_type=jnp.float32)
    total_rows = projected.shape[1]
    queries = (projected[0] + qkv_bias[0]).astype(jnp.bfloat16)
    key_rows = (projected[1] + qkv_bias[1]).astype(jnp.bfloat16)
    value_rows = (projected[2] + qkv_bias[2]).astype(jnp.bfloat16)
    head_q = queries.reshape(total_rows, heads_here, HEAD_DIM)
    head_k = key_rows.reshape(total_rows, heads_here, HEAD_DIM)
    head_v = value_rows.reshape(total_rows, heads_here, HEAD_DIM)
    scores = jnp.einsum(
        "qhe,khe->hqk", head_q, head_k, preferred_element_type=jnp.float32
    ) * HEAD_DIM ** (-0.5)
    pieces = prompt_pieces[0]
    position = jnp.arange(total_rows)
    allowed = (pieces[:, None] == pieces[None, :]) & (position[None, :] <= position[:, None])
    scores = jnp.where(allowed[None], scores, -1e30)
    highest = jnp.max(scores, axis=-1, keepdims=True)
    weights = jnp.exp(scores - highest)
    probs = (weights / jnp.sum(weights, axis=-1, keepdims=True)).astype(jnp.bfloat16)
    context = jnp.einsum("hqk,khe->qhe", probs, head_v, preferred_element_type=jnp.float32)
    context = context.reshape(total_rows, width).astype(jnp.bfloat16)
    attended = lax.psum_scatter(
        jnp.dot(context, out_weight, preferred_element_type=jnp.float32).astype(jnp.bfloat16),
        "tp",
        scatter_dimension=0,
        tiled=True,
    ).astype(jnp.float32)
    prompt_out = (prompt_rows.astype(jnp.float32) + attended + out_bias).astype(jnp.bfloat16)
    prompt_cache = jnp.stack([key_rows, value_rows])
    targets = migrate_to[:, 0]
    onehot = (targets[:, None] == jnp.arange(rep_count)[None, :]).astype(jnp.float32)
    lower = (jnp.arange(leaving)[:, None] > jnp.arange(leaving)[None, :]).astype(jnp.float32)
    earlier = jnp.dot(lower, onehot)
    rank = jnp.sum(earlier * onehot, axis=1).astype(jnp.int32)
    slot = targets * CAP + rank
    placing = (jnp.arange(slot_count)[:, None] == slot[None, :]).astype(jnp.bfloat16)
    cells = jnp.arange(length)
    live = cells[None, :] < request_ages[:, None]
    partial_value, updated = decode_partial(
        decode_rows,
        past_cache,
        live,
        request_ages,
        norm_gain,
        norm_bias,
        qkv_weight,
        qkv_bias,
        out_weight,
    )
    summed = lax.psum(partial_value.astype(jnp.bfloat16), "tp").astype(jnp.float32)
    decode_out = (decode_rows.astype(jnp.float32) + summed + out_bias).astype(jnp.bfloat16)
    kept_out = decode_out[:staying]
    kept_cache = updated[:staying]
    send_cache = jnp.einsum(
        "so,oklh->sklh", placing, updated[staying:], preferred_element_type=jnp.float32
    ).astype(jnp.bfloat16)
    send_rows = jnp.dot(placing, decode_out[staying:], preferred_element_type=jnp.float32).astype(
        jnp.bfloat16
    )
    moved_cache, moved_out = (
        lax.all_to_all(send_cache, "rep", split_axis=0, concat_axis=0, tiled=True),
        lax.all_to_all(send_rows, "rep", split_axis=0, concat_axis=0, tiled=True),
    )
    return (prompt_out, prompt_cache, kept_out, kept_cache, moved_out, moved_cache)


def solution(mesh):
    placed = (
        P(("rep", "tp"), None),
        P("rep", None),
        P("rep", None),
        P("rep"),
        P("rep", None),
        P("rep", None, None, "tp"),
        P(),
        P(),
        P(None, None, "tp"),
        P(None, "tp"),
        P("tp", None),
        P(),
    )
    return jax.shard_map(
        on_device,
        mesh=mesh,
        in_specs=placed,
        out_specs=(
            P(("rep", "tp"), None),
            P(None, "rep", "tp"),
            P("rep", None),
            P("rep", None, None, "tp"),
            P("rep", None),
            P("rep", None, None, "tp"),
        ),
        check_vma=False,
    )
```

profile of v0, /device:TPU:8, one launch (start us, length us, event | category | flops | bytes accessed | tf_op | source)
XLA Modules:
  0.0 225.0 jit_solution(8399299144730349695)
XLA Ops:
  7.2 0.7 all-gather.2.cloned.1.call-update
  8.0 0.8 iota_compare_fusion.1
  8.9 1.0 convert_reduce_fusion.1
  10.0 1.1 fusion.32
  11.1 1.6 convolution_bitcast_fusion
  13.1 5.5 %fusion.71 = (bf16[40,1,128,256]{3,2,1,0:T(8,128)(2,1)}, bf16[40,1,128,256]{3,2,1,0:T(8,128)(2,1)}) fusion(bf16[40,2,128,256]{3,2,1,0:T(8,128)(2,1)} %param.17), kind=kLoop, calls=%fused_computation.117 | loop fusion | bytes 10485760 | tf_op jit(solution)/shard_map/slice | solution.py:31
  18.6 4.4 %copy.84 = bf16[40,1,128,256]{2,3,0,1:T(8,128)(2,1)} copy(bf16[40,1,128,256]{3,2,1,0:T(8,128)(2,1)} %get-tuple-element.36) | data formatting | bytes 5242880 | tf_op jit(solution)/shard_map/reshape;squeeze | solution.py:31
  23.0 2.6 %fusion.53 = f32[40,2,1,128]{3,2,1,0:T(1,128)S(1)} fusion(bf16[40,128,2,128]{1,3,2,0:T(8,128)(2,1)} %bitcast.75, bf16[40,2,128,1]{2,1,0,3:T(2,128)(2,1)S(1)} %get-tuple-element.49), kind=kOutput, calls=%fused_computation.82 | convolution fusion | flops 2621440 | bytes 2682880 | tf_op jit(solution)/shard_map/rhe,rlhe->rhl/dot_general | solution.py:35
  26.1 4.9 %reshape.266 = bf16[40,128,2,128]{3,2,1,0:T(2,128)(2,1)} reshape(bf16[40,1,128,256]{3,2,1,0:T(8,128)(2,1)} %get-tuple-element.37) | data formatting | bytes 5242880 | tf_op jit(solution)/shard_map/reshape;squeeze | solution.py:32
  31.1 4.4 %fusion.11 = f32[40,2,1,128]{3,2,1,0:T(1,128)S(1)} fusion(bf16[40,2,128,1]{2,0,1,3:T(8,128)(2,1)S(1)} %fusion.59, bf16[40,128,2,128]{3,2,1,0:T(2,128)(2,1)} %reshape.266), kind=kOutput, calls=%fused_computation.20 | convolution fusion | flops 2621440 | bytes 2682880 | tf_op jit(solution)/shard_map/rhl,rlhe->rhe/dot_general | solution.py:52
  35.7 1.0 convolution_convert_fusion.2
  36.6 0.2 reduce-scatter.2.cloned.1.call-start
  36.9 0.3 fusion.29
  37.2 1.0 fusion.23
  38.3 8.5 %broadcast_select_fusion = (bf16[40,1,128,256]{3,0,2,1:T(8,128)(2,1)}, bf16[40,1,128,256]{3,0,2,1:T(8,128)(2,1)}) fusion(pred[40,128]{0,1:T(8,128)(4,1)S(1)} %get-tuple-element.57, bf16[40,256]{1,0:T(8,128)(2,1)S(1)} %get-tuple-element.43, bf16[40,1,128,256]{3,2,1,0:T(8,128)(2,1)} %get-tuple-element.37, bf16[40,1,128,256]{3,2,1,0:T(8,128)(2,1)} %get-tuple-element.36, ...), kind=kLoop, calls=%fused_computation.26 | loop fusion | flops 2621440 | bytes 10531840 | tf_op jit(solution)/shard_map/jit(_where)/select_n | solution.py:60
  46.8 8.3 %all-gather.2.cloned.1.call-done = bf16[640,2048]{1,0:T(8,128)(2,1)} async-done(((bf16[80,2048]{1,0:T(8,128)(2,1)}), bf16[640,2048]{1,0:T(8,128)(2,1)}) %all-gather.2.cloned.1.call-update) | async-done | bytes 2621456 | tf_op jit(solution)/shard_map/all_gather | solution.py:85
  55.1 2.3 %convert_reduce_fusion = f32[640]{0:T(1024)S(1)} fusion(bf16[640,2048]{1,0:T(8,128)(2,1)} %all-gather.2.cloned.1.call-done), kind=kLoop, calls=%fused_computation.2 | loop fusion | flops 2620800 | bytes 2624000 | tf_op jit(solution)/shard_map/reduce_sum | solution.py:13
  57.4 0.2 copy-done.3
  57.6 0.8 fusion.3
  58.4 3.1 %fusion.25 = f32[3,640,256]{1,2,0:T(8,128)S(1)} fusion(bf16[3,2048,256]{2,1,0:T(8,128)(2,1)S(1)} %copy-done, bf16[640,2048]{1,0:T(8,128)(2,1)S(1)} %copy-done.3, f32[2048]{0:T(1024)S(1)} %copy-done.12, f32[2048]{0:T(1024)S(1)} %copy-done.13, f32[640]{0:T(1024)S(1)} %add_rsqrt_fusion, f32[640]{0:T(1024)S(1)} %broadcast_multiply_fusion), kind=kOutput, calls=%fused_computation.39 | convolution fusion | flops 2021130240 | bytes 7754752 | tf_op jit(solution)/shard_map/rd,cde->cre/dot_general | solution.py:86
  61.5 0.2 add_convert_fusion.1
  61.7 0.2 copy.64
  62.0 0.2 copy.63
  62.2 0.6 fusion.38
  62.8 0.4 copy-done.10
  63.2 2.0 fusion.74
  65.2 0.5 fusion.28
  65.7 0.7 copy-done.5
  66.4 2.4 %convolution_convert_fusion = bf16[640,2048]{1,0:T(8,128)(2,1)} fusion(bf16[640,256]{0,1:T(8,128)(2,1)S(1)} %bitcast.78, bf16[256,2048]{1,0:T(8,128)(2,1)S(1)} %copy-done.5), kind=kOutput, calls=%fused_computation.14 | convolution fusion | flops 672399360 | bytes 3997696 | tf_op jit(solution)/shard_map/dot_general | solution.py:107
  68.9 60.0 %all-reduce.2.cloned.1.call-done = bf16[40,2048]{1,0:T(8,128)(2,1)} async-done(((bf16[40,2048]{1,0:T(8,128)(2,1)}), bf16[40,2048]{1,0:T(8,128)(2,1)}) %all-reduce.2.cloned.1.call-update) | async-done | bytes 163856 | tf_op jit(solution)/shard_map/psum | solution.py:134
  128.8 1.0 fusion.37
  129.8 0.7 copy-done.8
  130.5 0.3 fusion.18
  130.8 0.5 broadcast.160
  131.3 1.3 reduce.1
  132.6 1.6 reshape.267
  134.3 7.4 %all-to-all-start = ((bf16[32,2,1024]{2,1,0:T(2,128)(2,1)}), bf16[32,2,1024]{2,1,0:T(2,128)(2,1)S(1)}, u32[]{:S(2)}, u32[]{:S(2)}) async-start(bf16[32,2,1024]{2,1,0:T(2,128)(2,1)} %reshape.267), calls=%async_computation.1 | async-start | bytes 262144 | tf_op jit(solution)/shard_map/all_to_all | solution.py:146
  141.7 2.6 %convolution_convert_fusion.1 = bf16[32,2,128,256]{3,0,2,1:T(8,128)(2,1)S(1)} fusion(bf16[40,1,128,256]{3,0,2,1:T(8,128)(2,1)S(1)} %copy-done.2, bf16[40,1,128,256]{3,0,2,1:T(8,128)(2,1)} %get-tuple-element.51, s32[16]{0:T(128)S(1)} %convert_add_fusion.1), kind=kOutput, calls=%fused_computation.16 | convolution fusion | flops 73400832 | bytes 9437248 | tf_op jit(solution)/shard_map/so,oklh->sklh/dot_general | solution.py:138
  144.3 4.4 %copy.72 = bf16[32,2,128,256]{3,2,1,0:T(8,128)(2,1)} copy(bf16[32,2,128,256]{3,0,2,1:T(8,128)(2,1)S(1)} %convolution_convert_fusion.1) | data formatting | bytes 8388608 | tf_op jit(solution)/shard_map/convert_element_type | solution.py:140
  148.7 7.4 %all-to-all-start.1 = ((bf16[32,2,128,256]{3,2,1,0:T(8,128)(2,1)}), bf16[32,2,128,256]{3,2,1,0:T(8,128)(2,1)}, u32[]{:S(2)}, u32[]{:S(2)}) async-start(bf16[32,2,128,256]{3,2,1,0:T(8,128)(2,1)} %copy.72), calls=%async_computation.2 | async-start | bytes 8388608 | tf_op jit(solution)/shard_map/all_to_all | solution.py:145
  156.2 1.6 fusion.7
  157.8 2.4 %copy.74 = bf16[24,2,128,256]{3,2,1,0:T(8,128)(2,1)} copy(bf16[24,2,128,256]{3,0,2,1:T(8,128)(2,1)S(1)} %fusion.7) | data formatting | bytes 6291456
  160.1 0.6 slice.71
  160.9 0.7 copy.116
  161.6 49.1 %all-to-all-done.1 = bf16[32,2,128,256]{3,2,1,0:T(8,128)(2,1)} async-done(((bf16[32,2,128,256]{3,2,1,0:T(8,128)(2,1)}), bf16[32,2,128,256]{3,2,1,0:T(8,128)(2,1)}, u32[]{:S(2)}, u32[]{:S(2)}) %all-to-all-start.1) | async-done | bytes 4194336 | tf_op jit(solution)/shard_map/all_to_all | solution.py:145
  210.8 1.1 copy.73
  211.9 1.8 add_convert_fusion.2
  213.7 4.8 %copy.120 = bf16[32,2,128,256]{3,2,1,0:T(8,128)(2,1)} copy(bf16[32,2,128,256]{3,2,1,0:T(8,128)(2,1)} %all-to-all-done.1) | data formatting | bytes 8388608
  (60 shorter events, 1.4 us)
Async XLA Ops:
  7.2 4.0 %copy-start = (bf16[3,2048,256]{2,1,0:T(8,128)(2,1)S(1)}, bf16[3,2048,256]{2,1,0:T(8,128)(2,1)}, u32[]{:S(2)}) copy-start(bf16[3,2048,256]{2,1,0:T(8,128)(2,1)} %param.20) | copy-start | bytes 9437188
  7.2 5.7 %copy-start.15 = (f32[3,256]{1,0:T(4,128)S(1)}, f32[3,256]{1,0:T(4,128)}, u32[]{:S(2)}) copy-start(f32[3,256]{1,0:T(4,128)} %param.21) | copy-start | bytes 9220
  7.2 47.9 %all-gather.2.cloned.1.call-start = ((), (), s32[]{:S(2)}) async-start(), calls=%async_computation.3 | async-start | bytes 2949120 | tf_op jit(solution)/shard_map/all_gather | solution.py:85
  7.9 120.9 %all-reduce.2.cloned.1.call-start = ((), (), s32[]{:S(2)}) async-start(), calls=%async_computation.5 | async-start | bytes 327680 | tf_op jit(solution)/shard_map/psum | solution.py:134
  31.1 4.6 %copy-start.4 = (bf16[256,2048]{1,0:T(8,128)(2,1)S(1)}, bf16[256,2048]{1,0:T(8,128)(2,1)}, u32[]{:S(2)}) copy-start(bf16[256,2048]{1,0:T(8,128)(2,1)} %param.22) | copy-start | bytes 3145732
  31.1 5.8 %copy-start.16 = (s32[16,1]{0,1:T(1,128)S(1)}, s32[16,1]{0,1:T(1,128)}, u32[]{:S(2)}) copy-start(s32[16,1]{0,1:T(1,128)} %param.16) | copy-start | bytes 196
  31.1 6.1 %copy-start.14 = (s32[1,640]{1,0:T(1,128)S(1)}, s32[1,640]{1,0:T(1,128)}, u32[]{:S(2)}) copy-start(s32[1,640]{1,0:T(1,128)} %param.13) | copy-start | bytes 7684
  36.6 175.2 %reduce-scatter.2.cloned.1.call-start = ((), (), s32[]{:S(2)}) async-start(), calls=%async_computation.4 | async-start | bytes 2949120 | tf_op jit(solution)/shard_map/reduce_scatter | solution.py:106
  46.8 11.7 %copy-start.12 = (f32[2048]{0:T(1024)S(1)}, f32[2048]{0:T(1024)}, u32[]{:S(2)}) copy-start(f32[2048]{0:T(1024)} %param.19) | copy-start | bytes 24580
  55.1 2.5 %copy-start.3 = (bf16[640,2048]{1,0:T(8,128)(2,1)S(1)}, bf16[640,2048]{1,0:T(8,128)(2,1)}, u32[]{:S(2)}) copy-start(bf16[640,2048]{1,0:T(8,128)(2,1)} %all-gather.2.cloned.1.call-done) | copy-start | bytes 7864324
  55.1 3.4 %copy-start.13 = (f32[2048]{0:T(1024)S(1)}, f32[2048]{0:T(1024)}, u32[]{:S(2)}) copy-start(f32[2048]{0:T(1024)} %param.18) | copy-start | bytes 24580
  62.2 1.0 copy-start.10
  65.2 1.2 copy-start.5
  66.4 62.4 %copy-start.6 = (bf16[40,2048]{1,0:T(8,128)(2,1)S(1)}, bf16[40,2048]{1,0:T(8,128)(2,1)}, u32[]{:S(2)}) copy-start(bf16[40,2048]{1,0:T(8,128)(2,1)} %param.14) | copy-start | bytes 491524
  66.4 62.4 %copy-start.11 = (f32[2048]{0:T(1024)S(1)}, f32[2048]{0:T(1024)}, u32[]{:S(2)}) copy-start(f32[2048]{0:T(1024)} %param.23) | copy-start | bytes 24580
  68.8 72.9 %copy-start.2 = (bf16[40,1,128,256]{3,0,2,1:T(8,128)(2,1)S(1)}, bf16[40,1,128,256]{3,0,2,1:T(8,128)(2,1)}, u32[]{:S(2)}) copy-start(bf16[40,1,128,256]{3,0,2,1:T(8,128)(2,1)} %get-tuple-element.50) | copy-start | bytes 7864324
  129.8 0.7 copy-start.8
  134.3 14.5 %all-to-all-start = ((bf16[32,2,1024]{2,1,0:T(2,128)(2,1)}), bf16[32,2,1024]{2,1,0:T(2,128)(2,1)S(1)}, u32[]{:S(2)}, u32[]{:S(2)}) async-start(bf16[32,2,1024]{2,1,0:T(2,128)(2,1)} %reshape.267), calls=%async_computation.1 | async-start | bytes 262144 | tf_op jit(solution)/shard_map/all_to_all | solution.py:146
  148.7 62.0 %all-to-all-start.1 = ((bf16[32,2,128,256]{3,2,1,0:T(8,128)(2,1)}), bf16[32,2,128,256]{3,2,1,0:T(8,128)(2,1)}, u32[]{:S(2)}, u32[]{:S(2)}) async-start(bf16[32,2,128,256]{3,2,1,0:T(8,128)(2,1)} %copy.72), calls=%async_computation.2 | async-start | bytes 8388608 | tf_op jit(solution)/shard_map/all_to_all | solution.py:145
  157.8 2.4 %copy-start.9 = (bf16[40,2048]{1,0:T(8,128)(2,1)S(1)}, bf16[40,2048]{1,0:T(8,128)(2,1)}, u32[]{:S(2)}) copy-start(bf16[40,2048]{1,0:T(8,128)(2,1)} %copy-done.8) | copy-start | bytes 491524
  160.1 51.7 %copy-start.7 = (bf16[80,2048]{1,0:T(8,128)(2,1)S(1)}, bf16[80,2048]{1,0:T(8,128)(2,1)}, u32[]{:S(2)}) copy-start(bf16[80,2048]{1,0:T(8,128)(2,1)} %param.12) | copy-start | bytes 983044
  213.7 4.9 %copy-start.1 = (bf16[3,2048,256]{2,1,0:T(8,128)(2,1)S(1)}, bf16[3,2048,256]{2,1,0:T(8,128)(2,1)}, u32[]{:S(2)}) copy-start(bf16[3,2048,256]{2,1,0:T(8,128)(2,1)} %param.20) | copy-start | bytes 9437188
Sparse Core Ops, SparseCore 0:
  9.8 45.1 all-gather.1
  58.0 70.8 all-reduce.1
  131.6 42.1 reduce-scatter.1
where the time goes:
time: 226 us; the launch traced here: 225 us
  waiting for transfers between devices  118 us (52%)
  local copies, waits for them, and re-layouts  34.1 us (15%)
  other arithmetic  24.3 us (11%)
  matrix products  19.4 us (9%)
  starting transfers between devices  15.1 us (7%)
  between operations  14.1 us (6%)
    psum x1, waiting for transfers between devices, on_device(): lax.psum(partial_value.astype(jnp.bfloat16), 'tp').astype(jnp.float32)  60 us
    all_to_all x1, waiting for transfers between devices, on_device(): lax.all_to_all(send_cache, 'rep', split_axis=0, concat_axis=0, tiled=True)  49.1 us
    unnamed x40, local copies, waits for them, and re-layouts  12.8 us
    select_n x1, other arithmetic, decode_partial(): new_values = jnp.where(written, value_new[:, None, :], cache[:, 1])  8.49 us
    all_gather x1, waiting for transfers between devices, on_device(): lax.all_gather(prompt_rows, 'tp', axis=0, tiled=True)  8.31 us
    all_to_all x1, starting transfers between devices, on_device(): lax.all_to_all(send_cache, 'rep', split_axis=0, concat_axis=0, tiled=True)  7.44 us
    all_to_all x1, starting transfers between devices, on_device(): lax.all_to_all(send_rows, 'rep', split_axis=0, concat_axis=0, tiled=True)  7.41 us
    slice x1, local copies, waits for them, and re-layouts, decode_partial(): old_keys = cache[:, 0].reshape(count, length, heads_here, HEAD_DIM)  5.54 us
  transfers between devices with their start and end apart: 5, of which 3 were waited for; matrix products, arithmetic and copies ran while one was open for 31% of the time, Pallas kernels for 0%

commit v1 on v0

--- a/solution.py
+++ b/solution.py
@@ -1,3 +1,4 @@
+import functools
 import jax
 import jax.numpy as jnp
 from jax import lax
@@ -6,6 +7,21 @@
 HEAD_DIM = 128
 CAP = 1
 EPSILON = 1e-05
+
+
+def _wrap_slots(block_in, across):
+    n_axis = lax.axis_size(across)
+    shelf = []
+    to_i = 0
+    while to_i < block_in.ndim:
+        shelf.append(n_axis if to_i == 0 else 1)
+        to_i = to_i + 1
+    outer = jnp.tile(block_in, shelf)
+    res = lax.all_to_all(outer, across, split_axis=0, concat_axis=0, tiled=True)
+    return res
+
+
+stops_all_feed = functools.partial(_wrap_slots, across="tp")
 
 
 def layer_norm(values, norm_gain, norm_bias):
@@ -82,7 +98,7 @@
     leaving = migrate_to.shape[0]
     staying = decode_rows.shape[0] - leaving
     slot_count = rep_count * CAP
-    normed = layer_norm(lax.all_gather(prompt_rows, "tp", axis=0, tiled=True), norm_gain, norm_bias)
+    normed = layer_norm(stops_all_feed(prompt_rows), norm_gain, norm_bias)
     projected = jnp.einsum("rd,cde->cre", normed, qkv_weight, preferred_element_type=jnp.float32)
     total_rows = projected.shape[1]
     queries = (projected[0] + qkv_bias[0]).astype(jnp.bfloat16)

time: 226 us -> 230 us (1.018)
  waiting for transfers between devices: 118 us -> 99.9 us
  starting transfers between devices: 15.1 us -> 23.7 us
  other arithmetic: 24.3 us -> 32.7 us
  local copies, waits for them, and re-layouts: 34.1 us -> 40.3 us
    psum x1, waiting for transfers between devices: 60 us -> 33.5 us  [on_device(): lax.psum(partial_value.astype(jnp.bfloat16), 'tp').astype(jnp.float32)]
    all_to_all x0 -> x1, waiting for transfers between devices: none -> 17.3 us  [_wrap_slots(): res = lax.all_to_all(outer, across, split_axis=0, concat_axis=0, tiled=True)]
    all_to_all x0 -> x1, starting transfers between devices: none -> 8.61 us  [_wrap_slots(): res = lax.all_to_all(outer, across, split_axis=0, concat_axis=0, tiled=True)]
    all_gather x1 -> x0, waiting for transfers between devices: 8.31 us -> none  [on_device(): lax.all_gather(prompt_rows, 'tp', axis=0, tiled=True)]
    another operation x0 -> x1, local copies, waits for them, and re-layouts: none -> 2.94 us  [_wrap_slots(): outer = jnp.tile(block_in, shelf)]
    convert_element_type x0 -> x1, other arithmetic: none -> 2.78 us  [layer_norm(): return (scaled * norm_gain + norm_bias).astype(jnp.bfloat16)]
    unnamed x40 -> x48, local copies, waits for them, and re-layouts: 12.8 us -> 10.7 us
  transfers between devices with their start and end apart: 5 -> 5, of which waited for: 3 -> 3; matrix products, arithmetic and copies ran while one was open for 31% -> 35% of each run, Pallas kernels for 0% -> 0%
where the time goes in v1:
time: 230 us; the launch traced here: 229 us
  waiting for transfers between devices  99.9 us (43%)
  local copies, waits for them, and re-layouts  40.3 us (18%)
  other arithmetic  32.7 us (14%)
  starting transfers between devices  23.7 us (10%)
  matrix products  18 us (8%)
  between operations  14.4 us (6%)
    all_to_all x1, waiting for transfers between devices, on_device(): lax.all_to_all(send_cache, 'rep', split_axis=0, concat_axis=0, tiled=True)  49.1 us
    psum x1, waiting for transfers between devices, on_device(): lax.psum(partial_value.astype(jnp.bfloat16), 'tp').astype(jnp.float32)  33.5 us
    all_to_all x1, waiting for transfers between devices, _wrap_slots(): res = lax.all_to_all(outer, across, split_axis=0, concat_axis=0, tiled=True)  17.3 us
    unnamed x48, local copies, waits for them, and re-layouts  10.7 us
    all_to_all x1, starting transfers between devices, _wrap_slots(): res = lax.all_to_all(outer, across, split_axis=0, concat_axis=0, tiled=True)  8.61 us
    select_n x1, other arithmetic, decode_partial(): new_values = jnp.where(written, value_new[:, None, :], cache[:, 1])  8.4 us
    all_to_all x1, starting transfers between devices, on_device(): lax.all_to_all(send_cache, 'rep', split_axis=0, concat_axis=0, tiled=True)  7.44 us
    all_to_all x1, starting transfers between devices, on_device(): lax.all_to_all(send_rows, 'rep', split_axis=0, concat_axis=0, tiled=True)  7.4 us
  transfers between devices with their start and end apart: 5, of which 3 were waited for; matrix products, arithmetic and copies ran while one was open for 35% of the time, Pallas kernels for 0%

profile of v1, /device:TPU:8, one launch (start us, length us, event | category | flops | bytes accessed | tf_op | source)
XLA Modules:
  0.0 229.0 jit_solution(17110308166304728449)
XLA Ops:
  7.2 2.9 %tile.2 = bf16[8,80,2048]{2,1,0:T(8,128)(2,1)} broadcast(bf16[80,2048]{1,0:T(8,128)(2,1)} %param.12), dimensions={1,2} | broadcast | bytes 2949120 | tf_op jit(solution)/shard_map/tile | solution.py:19
  10.1 8.6 %all-to-all-start = ((bf16[8,80,2048]{2,1,0:T(8,128)(2,1)}), bf16[8,80,2048]{2,1,0:T(8,128)(2,1)}, u32[]{:S(2)}, u32[]{:S(2)}) async-start(bf16[8,80,2048]{2,1,0:T(8,128)(2,1)} %tile.2), calls=%async_computation | async-start | bytes 5242880 | tf_op jit(solution)/shard_map/all_to_all | solution.py:20
  19.2 0.6 iota_compare_fusion.1
  19.9 0.7 convolution_bitcast_fusion
  20.6 0.7 fusion.65
  21.3 0.8 squeeze.31
  22.1 1.4 squeeze.30
  23.5 0.6 fusion.66
  24.1 1.5 multiply_reduce_fusion.1
  25.6 1.4 copy.68
  27.0 5.6 %fusion.64 = (bf16[40,1,128,256]{3,2,1,0:T(8,128)(2,1)}, bf16[40,1,128,256]{3,2,1,0:T(8,128)(2,1)}) fusion(bf16[40,2,128,256]{3,2,1,0:T(8,128)(2,1)} %param.17), kind=kLoop, calls=%fused_computation.112 | loop fusion | bytes 10485760 | tf_op jit(solution)/shard_map/slice | solution.py:47
  32.5 4.4 %copy.84 = bf16[40,1,128,256]{2,3,0,1:T(8,128)(2,1)} copy(bf16[40,1,128,256]{3,2,1,0:T(8,128)(2,1)} %get-tuple-element.36) | data formatting | bytes 5242880 | tf_op jit(solution)/shard_map/reshape;squeeze | solution.py:47
  36.9 2.5 %fusion.46 = f32[40,2,1,128]{3,2,1,0:T(1,128)S(1)} fusion(bf16[40,128,2,128]{1,3,2,0:T(8,128)(2,1)} %bitcast.85, bf16[40,2,128,1]{2,1,0,3:T(2,128)(2,1)S(1)} %get-tuple-element.49), kind=kOutput, calls=%fused_computation.77 | convolution fusion | flops 2621440 | bytes 2682880 | tf_op jit(solution)/shard_map/rhe,rlhe->rhl/dot_general | solution.py:51
  39.5 0.7 multiply_maximum_fusion
  40.4 1.3 fusion.58
  41.7 0.8 copy.70
  42.4 4.9 %reshape.296 = bf16[40,128,2,128]{3,2,1,0:T(2,128)(2,1)} reshape(bf16[40,1,128,256]{3,2,1,0:T(8,128)(2,1)} %get-tuple-element.37) | data formatting | bytes 5242880 | tf_op jit(solution)/shard_map/reshape;squeeze | solution.py:48
  47.3 0.8 fusion.52
  48.2 4.4 %fusion.8 = f32[40,2,1,128]{3,2,1,0:T(1,128)S(1)} fusion(bf16[40,2,128,1]{2,0,1,3:T(8,128)(2,1)S(1)} %fusion.52, bf16[40,128,2,128]{3,2,1,0:T(2,128)(2,1)} %reshape.296), kind=kOutput, calls=%fused_computation.18 | convolution fusion | flops 2621440 | bytes 2682880 | tf_op jit(solution)/shard_map/rhl,rlhe->rhe/dot_general | solution.py:68
  52.7 1.0 convolution_convert_fusion.2
  54.2 1.0 fusion.16
  55.3 8.4 %broadcast_select_fusion = (bf16[40,1,128,256]{3,0,2,1:T(8,128)(2,1)}, bf16[40,1,128,256]{3,0,2,1:T(8,128)(2,1)}) fusion(pred[40,128]{0,1:T(8,128)(4,1)S(1)} %copy-done.8, bf16[40,256]{1,0:T(8,128)(2,1)S(1)} %get-tuple-element.43, bf16[40,1,128,256]{3,2,1,0:T(8,128)(2,1)} %get-tuple-element.37, bf16[40,1,128,256]{3,2,1,0:T(8,128)(2,1)} %get-tuple-element.36, ...), kind=kLoop, calls=%fused_computation.21 | loop fusion | flops 2621440 | bytes 10531840 | tf_op jit(solution)/shard_map/jit(_where)/select_n | solution.py:76
  63.7 17.3 %all-to-all-done = bf16[8,80,2048]{2,1,0:T(8,128)(2,1)} async-done(((bf16[8,80,2048]{2,1,0:T(8,128)(2,1)}), bf16[8,80,2048]{2,1,0:T(8,128)(2,1)}, u32[]{:S(2)}, u32[]{:S(2)}) %all-to-all-start) | async-done | bytes 2621472 | tf_op jit(solution)/shard_map/all_to_all | solution.py:20
  81.0 2.2 convert_reduce_fusion
  83.2 2.6 %multiply_reduce_fusion = f32[8,80]{1,0:T(8,128)S(1)} fusion(bf16[8,80,2048]{2,1,0:T(8,128)(2,1)} %all-to-all-done, f32[8,80]{1,0:T(8,128)S(1)} %broadcast_multiply_fusion), kind=kLoop, calls=%fused_computation.8 | loop fusion | flops 5242240 | bytes 2626560 | tf_op jit(solution)/shard_map/reduce_sum | solution.py:30
  85.9 2.8 %fusion.4 = bf16[640,2048]{1,0:T(8,128)(2,1)S(1)} fusion(bf16[8,80,2048]{2,1,0:T(8,128)(2,1)} %all-to-all-done, f32[2048]{0:T(1024)S(1)} %copy-done.9, f32[2048]{0:T(1024)S(1)} %copy-done.11, f32[640]{0:T(1024)S(1)} %rsqrt.20, f32[640]{0:T(1024)S(1)} %div.38), kind=kLoop, calls=%fused_computation.7 | loop fusion | flops 7864320 | bytes 5264384 | tf_op jit(solution)/shard_map/convert_element_type | solution.py:32
  88.7 2.8 %fusion.18 = f32[3,640,256]{1,2,0:T(8,128)S(1)} fusion(bf16[3,2048,256]{2,1,0:T(8,128)(2,1)S(1)} %copy-done, bf16[640,2048]{1,0:T(8,128)(2,1)S(1)} %fusion.4), kind=kOutput, calls=%fused_computation.34 | convolution fusion | flops 2013265920 | bytes 7733248 | tf_op jit(solution)/shard_map/rd,cde->cre/dot_general | solution.py:102
  91.5 0.9 add_convert_fusion.1
  92.9 0.6 fusion.31
  93.5 4.0 %fusion.67 = (f32[2,640]{1,0:T(2,128)S(1)}, f32[2,640,640]{1,2,0:T(8,128)S(1)}) fusion(f32[2,640,640]{1,2,0:T(8,128)S(1)} %fusion.31, pred[640,640]{0,1:T(8,128)(4,1)} %fusion.16), kind=kOutput, calls=%fused_computation.115 | output fusion | flops 4915839 | bytes 6968320 | tf_op jit(solution)/shard_map/sub | solution.py:118
  98.1 0.7 copy-done.4
  98.8 2.4 %convolution_convert_fusion = bf16[640,2048]{1,0:T(8,128)(2,1)} fusion(bf16[640,256]{0,1:T(8,128)(2,1)S(1)} %bitcast.88, bf16[256,2048]{1,0:T(8,128)(2,1)S(1)} %copy-done.4), kind=kOutput, calls=%fused_computation.12 | convolution fusion | flops 672399360 | bytes 3997696 | tf_op jit(solution)/shard_map/dot_general | solution.py:123
  101.2 33.5 %all-reduce.2.cloned.1.call-done = bf16[40,2048]{1,0:T(8,128)(2,1)} async-done(((bf16[40,2048]{1,0:T(8,128)(2,1)}), bf16[40,2048]{1,0:T(8,128)(2,1)}) %all-reduce.2.cloned.1.call-update) | async-done | bytes 163856 | tf_op jit(solution)/shard_map/psum | solution.py:150
  134.7 1.0 fusion.30
  136.5 0.7 reduce.3
  137.2 0.7 reshape.297
  137.9 7.4 %all-to-all-start.1 = ((bf16[32,2,1024]{2,1,0:T(2,128)(2,1)}), bf16[32,2,1024]{2,1,0:T(2,128)(2,1)S(1)}, u32[]{:S(2)}, u32[]{:S(2)}) async-start(bf16[32,2,1024]{2,1,0:T(2,128)(2,1)} %reshape.297), calls=%async_computation.2 | async-start | bytes 262144 | tf_op jit(solution)/shard_map/all_to_all | solution.py:162
  145.4 2.6 %convolution_convert_fusion.1 = bf16[32,2,128,256]{3,0,2,1:T(8,128)(2,1)S(1)} fusion(bf16[40,1,128,256]{3,0,2,1:T(8,128)(2,1)S(1)} %copy-done.2, bf16[40,1,128,256]{3,0,2,1:T(8,128)(2,1)} %get-tuple-element.51, s32[16]{0:T(128)S(1)} %convert_add_fusion.1), kind=kOutput, calls=%fused_computation.14 | convolution fusion | flops 73400832 | bytes 9437248 | tf_op jit(solution)/shard_map/so,oklh->sklh/dot_general | solution.py:154
  148.0 4.4 %copy.72 = bf16[32,2,128,256]{3,2,1,0:T(8,128)(2,1)} copy(bf16[32,2,128,256]{3,0,2,1:T(8,128)(2,1)S(1)} %convolution_convert_fusion.1) | data formatting | bytes 8388608 | tf_op jit(solution)/shard_map/convert_element_type | solution.py:156
  152.4 7.4 %all-to-all-start.2 = ((bf16[32,2,128,256]{3,2,1,0:T(8,128)(2,1)}), bf16[32,2,128,256]{3,2,1,0:T(8,128)(2,1)}, u32[]{:S(2)}, u32[]{:S(2)}) async-start(bf16[32,2,128,256]{3,2,1,0:T(8,128)(2,1)} %copy.72), calls=%async_computation.3 | async-start | bytes 8388608 | tf_op jit(solution)/shard_map/all_to_all | solution.py:161
  159.8 1.6 fusion.5
  161.4 2.4 %copy.74 = bf16[24,2,128,256]{3,2,1,0:T(8,128)(2,1)} copy(bf16[24,2,128,256]{3,0,2,1:T(8,128)(2,1)S(1)} %fusion.5) | data formatting | bytes 6291456
  163.8 0.6 slice.71
  164.6 0.7 copy.116
  165.3 49.1 %all-to-all-done.2 = bf16[32,2,128,256]{3,2,1,0:T(8,128)(2,1)} async-done(((bf16[32,2,128,256]{3,2,1,0:T(8,128)(2,1)}), bf16[32,2,128,256]{3,2,1,0:T(8,128)(2,1)}, u32[]{:S(2)}, u32[]{:S(2)}) %all-to-all-start.2) | async-done | bytes 4194336 | tf_op jit(solution)/shard_map/all_to_all | solution.py:161
  214.5 1.1 copy.73
  215.5 1.8 add_convert_fusion.2
  217.3 4.8 %copy.120 = bf16[32,2,128,256]{3,2,1,0:T(8,128)(2,1)} copy(bf16[32,2,128,256]{3,2,1,0:T(8,128)(2,1)} %all-to-all-done.2) | data formatting | bytes 8388608
  (71 shorter events, 3.7 us)
Async XLA Ops:
  7.2 12.7 %copy-start = (bf16[3,2048,256]{2,1,0:T(8,128)(2,1)S(1)}, bf16[3,2048,256]{2,1,0:T(8,128)(2,1)}, u32[]{:S(2)}) copy-start(bf16[3,2048,256]{2,1,0:T(8,128)(2,1)} %param.20) | copy-start | bytes 9437188
  10.1 8.7 %copy-start.5 = (bf16[40,2048]{1,0:T(8,128)(2,1)S(1)}, bf16[40,2048]{1,0:T(8,128)(2,1)}, u32[]{:S(2)}) copy-start(bf16[40,2048]{1,0:T(8,128)(2,1)} %param.14) | copy-start | bytes 491524
  10.1 9.0 %copy-start.19 = (s32[40]{0:T(128)S(1)}, s32[40]{0:T(128)}, u32[]{:S(2)}) copy-start(s32[40]{0:T(128)} %param.15) | copy-start | bytes 484
  10.1 9.8 %copy-start.9 = (f32[2048]{0:T(1024)S(1)}, f32[2048]{0:T(1024)}, u32[]{:S(2)}) copy-start(f32[2048]{0:T(1024)} %param.19) | copy-start | bytes 24580
  10.1 9.8 %copy-start.10 = (f32[2048]{0:T(1024)S(1)}, f32[2048]{0:T(1024)}, u32[]{:S(2)}) copy-start(f32[2048]{0:T(1024)} %param.18) | copy-start | bytes 24580
  10.1 70.9 %all-to-all-start = ((bf16[8,80,2048]{2,1,0:T(8,128)(2,1)}), bf16[8,80,2048]{2,1,0:T(8,128)(2,1)}, u32[]{:S(2)}, u32[]{:S(2)}) async-start(bf16[8,80,2048]{2,1,0:T(8,128)(2,1)} %tile.2), calls=%async_computation | async-start | bytes 5242880 | tf_op jit(solution)/shard_map/all_to_all | solution.py:20
  18.7 4.8 %copy-start.18 = (f32[3,256]{1,0:T(4,128)S(1)}, f32[3,256]{1,0:T(4,128)}, u32[]{:S(2)}) copy-start(f32[3,256]{1,0:T(4,128)} %param.21) | copy-start | bytes 9220
  18.7 116.0 %all-reduce.2.cloned.1.call-start = ((), (), s32[]{:S(2)}) async-start(), calls=%async_computation.5 | async-start | bytes 327680 | tf_op jit(solution)/shard_map/psum | solution.py:150
  24.1 1.5 copy-start.15
  40.2 1.4 copy-start.14
  48.1 4.4 %copy-start.13 = (f32[1,256]{1,0:T(1,128)S(1)}, f32[1,256]{1,0:T(1,128)}, u32[]{:S(2)}) copy-start(f32[1,256]{1,0:T(1,128)} %get-tuple-element.52) | copy-start | bytes 3076
  48.1 4.5 %copy-start.3 = (bf16[256,2048]{1,0:T(8,128)(2,1)S(1)}, bf16[256,2048]{1,0:T(8,128)(2,1)}, u32[]{:S(2)}) copy-start(bf16[256,2048]{1,0:T(8,128)(2,1)} %param.22) | copy-start | bytes 3145732
  48.1 5.8 %copy-start.17 = (s32[1,640]{1,0:T(1,128)S(1)}, s32[1,640]{1,0:T(1,128)}, u32[]{:S(2)}) copy-start(s32[1,640]{1,0:T(1,128)} %param.13) | copy-start | bytes 7684
  48.1 5.8 %copy-start.20 = (s32[16,1]{0,1:T(1,128)S(1)}, s32[16,1]{0,1:T(1,128)}, u32[]{:S(2)}) copy-start(s32[16,1]{0,1:T(1,128)} %param.16) | copy-start | bytes 196
  48.1 7.1 %copy-start.8 = (pred[40,128]{0,1:T(8,128)(4,1)S(1)}, pred[40,128]{0,1:T(8,128)(4,1)}, u32[]{:S(2)}) copy-start(pred[40,128]{0,1:T(8,128)(4,1)} %get-tuple-element.57) | copy-start | bytes 15364
  53.7 161.9 %reduce-scatter.2.cloned.1.call-start = ((), (), s32[]{:S(2)}) async-start(), calls=%async_computation.4 | async-start | bytes 2949120 | tf_op jit(solution)/shard_map/reduce_scatter | solution.py:122
  63.7 22.2 %copy-start.11 = (f32[2048]{0:T(1024)S(1)}, f32[2048]{0:T(1024)}, u32[]{:S(2)}) copy-start(f32[2048]{0:T(1024)} %param.18) | copy-start | bytes 24580
  91.5 1.4 copy-start.16
  97.6 1.2 copy-start.4
  98.8 35.9 %copy-start.12 = (f32[2048]{0:T(1024)S(1)}, f32[2048]{0:T(1024)}, u32[]{:S(2)}) copy-start(f32[2048]{0:T(1024)} %param.23) | copy-start | bytes 24580
  101.2 44.2 %copy-start.2 = (bf16[40,1,128,256]{3,0,2,1:T(8,128)(2,1)S(1)}, bf16[40,1,128,256]{3,0,2,1:T(8,128)(2,1)}, u32[]{:S(2)}) copy-start(bf16[40,1,128,256]{3,0,2,1:T(8,128)(2,1)} %get-tuple-element.50) | copy-start | bytes 7864324
  137.9 14.5 %all-to-all-start.1 = ((bf16[32,2,1024]{2,1,0:T(2,128)(2,1)}), bf16[32,2,1024]{2,1,0:T(2,128)(2,1)S(1)}, u32[]{:S(2)}, u32[]{:S(2)}) async-start(bf16[32,2,1024]{2,1,0:T(2,128)(2,1)} %reshape.297), calls=%async_computation.2 | async-start | bytes 262144 | tf_op jit(solution)/shard_map/all_to_all | solution.py:162
  152.4 62.0 %all-to-all-start.2 = ((bf16[32,2,128,256]{3,2,1,0:T(8,128)(2,1)}), bf16[32,2,128,256]{3,2,1,0:T(8,128)(2,1)}, u32[]{:S(2)}, u32[]{:S(2)}) async-start(bf16[32,2,128,256]{3,2,1,0:T(8,128)(2,1)} %copy.72), calls=%async_computation.3 | async-start | bytes 8388608 | tf_op jit(solution)/shard_map/all_to_all | solution.py:161
  161.4 53.0 %copy-start.6 = (bf16[1,640,256]{1,2,0:T(8,128)(2,1)S(1)}, bf16[1,640,256]{1,2,0:T(8,128)(2,1)}, u32[]{:S(2)}) copy-start(bf16[1,640,256]{1,2,0:T(8,128)(2,1)} %get-tuple-element.39) | copy-start | bytes 983044
  163.8 51.7 %copy-start.7 = (bf16[80,2048]{1,0:T(8,128)(2,1)S(1)}, bf16[80,2048]{1,0:T(8,128)(2,1)}, u32[]{:S(2)}) copy-start(bf16[80,2048]{1,0:T(8,128)(2,1)} %param.12) | copy-start | bytes 983044
  217.3 4.9 %copy-start.1 = (bf16[3,2048,256]{2,1,0:T(8,128)(2,1)S(1)}, bf16[3,2048,256]{2,1,0:T(8,128)(2,1)}, u32[]{:S(2)}) copy-start(bf16[3,2048,256]{2,1,0:T(8,128)(2,1)} %param.20) | copy-start | bytes 9437188
Sparse Core Ops, SparseCore 0:
  53.8 80.9 all-reduce.1
  137.5 42.1 reduce-scatter.1
